TPU v7x, 512 devices: a whole 4x8x8 slice. The times are simulated.
512 devices in a mesh: req: 128 (over z, y, core), grp: 4 (over x).
Axes of the slice: x: 4, y: 8, z: 8, core: 2. Of those that a mesh axis runs over, the one named last changes fastest.
Arguments:
- owner_slab: bfloat16 [65536, 1024], P('req'), may hold values from -6 to 6
- segment_ids: int32 [128, 512], P('req'), may hold values from 0 to 511, as said below
- head_weights: bfloat16 [1024, 16, 192], P(None, 'grp')
- merge_weights: bfloat16 [16, 64, 1024], P('grp'), may hold values from -0.1875 to 0.1875
- first_gain: float32 [1024], replicated, may hold values from 0.25 to 1.75
- first_bias: float32 [1024], replicated, may hold values from -3 to 3
- up_weights: bfloat16 [1024, 4096], P('req', 'grp'), may hold values from -0.1875 to 0.1875
- down_weights: bfloat16 [4096, 1024], P('grp', 'req'), may hold values from -0.09375 to 0.09375
- second_gain: float32 [1024], replicated, may hold values from 0.25 to 1.75
- second_bias: float32 [1024], replicated, may hold values from -3 to 3
- page_table: int32 [128, 4], P('req'), may hold values from 0 to 3, each once within a row
- row_map: int32 [128, 4, 128], P('req', 'grp'), may hold values from 0 to 127, each once within a row
Outputs:
- layer_out: bfloat16 [65536, 1024], P(('req', 'grp'))
- cache_pages: bfloat16 [512, 128, 16, 128], P('req', None, 'grp')
Inputs may be any that keep to these rules, and one draw needn't show every extreme that they name: `segment_ids`: within each slab the ids start at 0, never fall and rise by at most one from row to row; in one slab all 512 rows form a single request, and in one other slab every row is a request of its own.
All inputs are finite; a program needn't handle non-finite values.
Results may differ from a plain program's by a relative error of at most 0.0075.
Values may be sent and summed in bfloat16 or wider, within the bound.
No kernel may reach another device: no remote copies, remote signals or barrier semaphores. Data moves between devices by JAX's collectives and lax.ppermute only.
A program may use at most 64 MiB of HBM per device.

v0:
```python
import math
import jax
import jax.numpy as jnp
from jax import lax
from jax.sharding import PartitionSpec as P

EPSILON = 1e-05


def layer_norm(values, gain, bias):
    center = values - jnp.mean(values, axis=-1, keepdims=True)
    spread = jnp.mean(center * center, axis=-1, keepdims=True)
    return center * lax.rsqrt(spread + EPSILON) * gain + bias


def local(
    owner_slab,
    segment_ids,
    head_weights,
    merge_weights,
    first_gain,
    first_bias,
    up_weights,
    down_weights,
    second_gain,
    second_bias,
    page_table,
    row_map,
):
    group = lax.axis_size("grp")
    owners = lax.axis_size("req")
    rows_all = owner_slab.shape[0]
    width = owner_slab.shape[1]
    quarter = rows_all // group
    local_heads = head_weights.shape[1]
    head_dim = head_weights.shape[2] // 3
    projected = jnp.einsum(
        "nd,dhc->nhc", owner_slab, head_weights, preferred_element_type=jnp.float32
    ).astype(jnp.bfloat16)
    queries = jnp.moveaxis(projected[:, :, :head_dim], 1, 0)
    key_rows = jnp.moveaxis(projected[:, :, head_dim : 2 * head_dim], 1, 0)
    value_rows = jnp.moveaxis(projected[:, :, 2 * head_dim :], 1, 0)
    segment = segment_ids[0]
    position = jnp.arange(rows_all, dtype=jnp.int32)
    allowed = (position[:, None] >= position[None, :]) & (segment[:, None] == segment[None, :])
    scale = 1.0 / math.sqrt(head_dim)

    def one_head(operands):
        query_head, key_head, value_head = operands
        scores = (
            lax.dot_general(
                query_head, key_head, (((1,), (1,)), ((), ())), preferred_element_type=jnp.float32
            )
            * scale
        )
        scores = jnp.where(allowed, scores, -1e30)
        probs = jax.nn.softmax(scores, axis=-1).astype(jnp.bfloat16)
        return jnp.dot(probs, value_head, preferred_element_type=jnp.float32).astype(jnp.bfloat16)

    attended = jnp.moveaxis(lax.map(one_head, (queries, key_rows, value_rows)), 0, 1)
    own = lax.axis_index("grp")
    own_rows = lax.dynamic_slice_in_dim(owner_slab, own * quarter, quarter, 0).astype(jnp.float32)
    partial_rows = jnp.einsum(
        "nhd,hde->ne", attended, merge_weights, preferred_element_type=jnp.float32
    )
    mixed = lax.psum_scatter(partial_rows, "grp", scatter_dimension=0, tiled=True)
    hidden = layer_norm(own_rows + mixed, first_gain, first_bias).astype(jnp.bfloat16)
    slots = quarter // owners
    placed = jnp.zeros_like(hidden).at[row_map[0, 0]].set(hidden)
    arrived = lax.all_to_all(
        placed.reshape(owners, slots, width), "req", split_axis=0, concat_axis=0, tiled=True
    )
    even_rows = arrived.reshape(quarter, width)
    group_rows = lax.all_gather(even_rows, "grp", axis=0, tiled=True)
    raised = jnp.dot(
        group_rows,
        lax.all_gather(up_weights, "req", axis=0, tiled=True),
        preferred_element_type=jnp.float32,
    )
    activated = jax.nn.gelu(raised, approximate=False).astype(jnp.bfloat16)
    lowered_all = jnp.dot(
        activated,
        lax.all_gather(down_weights, "req", axis=1, tiled=True),
        preferred_element_type=jnp.float32,
    )
    lowered = lax.psum_scatter(lowered_all, "grp", scatter_dimension=0, tiled=True)
    layer_out = layer_norm(
        even_rows.astype(jnp.float32) + lowered, second_gain, second_bias
    ).astype(jnp.bfloat16)
    page_count = page_table.shape[1]
    page_rows = rows_all // page_count
    stacked = projected[:, :, head_dim:].reshape(page_count, page_rows, local_heads, 2 * head_dim)
    cache_pages = jnp.zeros_like(stacked).at[page_table[0]].set(stacked)
    return (layer_out, cache_pages)


def solution(mesh):
    in_specs = (
        P("req", None),
        P("req", None),
        P(None, "grp", None),
        P("grp", None, None),
        P(),
        P(),
        P("req", "grp"),
        P("grp", "req"),
        P(),
        P(),
        P("req", None),
        P("req", "grp", None),
    )
    out_specs = (P(("req", "grp"), None), P("req", None, "grp", None))
    return jax.shard_map(local, mesh=mesh, in_specs=in_specs, out_specs=out_specs, check_vma=False)
```

profile of v0, /device:TPU:1, one launch (start us, length us, event | category | flops | bytes accessed | tf_op | source)
XLA Modules:
  0.0 281.3 jit_solution(15280526608803334837)
XLA Ops:
  8.1 1.3 copy-done
  9.4 2.2 fusion.105
  11.7 0.1 convert_element_type.25
  11.8 0.1 slice_bitcast_fusion
  11.9 0.5 copy-done.7
  12.3 3.7 %while.11 = (s32[]{:T(128)}, bf16[4,512,64]{1,2,0:T(8,128)(2,1)S(1)}, bf16[4,512,64]{1,2,0:T(8,128)(2,1)S(1)}, bf16[4,512,64]{1,2,0:T(8,128)(2,1)S(1)}, bf16[4,5...) while((s32[]{:T(128)}, bf16[4,512,64]{1,2,0:T(8,128)(2,1)S(1)}, ...), condition=%wide.region_3.4_spmd.clone, body=%wide.region_0.3_spmd.clone.sunk | while | flops 70024192 | bytes 3424341 | solution.py:60
  12.3 0.4 fusion.116
  12.7 0.2 fusion.117
  12.9 0.3 fusion.118
  13.3 0.4 fusion.116
  13.7 0.2 fusion.117
  13.9 0.3 fusion.118
  14.2 0.4 fusion.116
  14.6 0.2 fusion.117
  14.8 0.3 fusion.118
  15.1 0.4 fusion.116
  15.6 0.2 fusion.117
  15.8 0.3 fusion.118
  16.1 0.7 copy-done.10
  16.8 3.0 %convolution_bitcast_fusion = f32[512,1024]{1,0:T(8,128)} fusion(bf16[4,64,1024]{2,1,0:T(8,128)(2,1)} %param.17, bf16[4,512,64]{1,2,0:T(8,128)(2,1)} %copy-done.10), kind=kOutput, calls=%fused_computation.40 | convolution fusion | flops 268435456 | bytes 2883584 | tf_op jit(solution)/shard_map/nhd,hde->ne/dot_general | solution.py:63
  19.8 0.0 all-gather.5.cloned.1.call-start
  19.9 0.5 all-gather.5.cloned.1.call-update
  20.4 0.5 all-gather.7.cloned.1.call-update
  21.1 39.4 %reduce-scatter.3.cloned.1.call-done = f32[128,1024]{1,0:T(8,128)} async-done(((f32[512,1024]{1,0:T(8,128)}), f32[128,1024]{1,0:T(8,128)}) %reduce-scatter.3.cloned.1.call-update) | async-done | bytes 524304 | tf_op jit(solution)/shard_map/reduce_scatter | solution.py:66
  60.4 1.2 fusion.70
  61.6 1.2 multiply_reduce_fusion.1
  62.9 1.9 scatter_custom_fusion
  64.8 0.5 broadcast.106
  65.3 0.8 reduce
  66.1 0.2 reshape.126
  66.3 30.1 %all_to_all.5 = bf16[128,2,512]{2,1,0:T(2,128)(2,1)S(1)} all-to-all(bf16[128,2,512]{2,1,0:T(2,128)(2,1)S(1)} %reshape.126), channel_id=1, replica_groups=mesh['req'=128,'grp'=4] {'req'}, dimensions={0} | all-to-all | bytes 524288 | tf_op jit(solution)/shard_map/all_to_all | solution.py:70
  96.4 0.2 reshape.127
  96.6 0.8 copy.29
  97.4 0.2 reduce-scatter.5.cloned.1.call-start
  97.7 16.5 %all-gather.5.cloned.1.call-done = bf16[1024,1024]{1,0:T(8,128)(2,1)} async-done(((bf16[8,1024]{1,0:T(8,128)(2,1)}), bf16[1024,1024]{1,0:T(8,128)(2,1)}) %all-gather.5.cloned.1.call-update) | async-done | bytes 2097168 | tf_op jit(solution)/shard_map/all_gather | solution.py:77
  114.2 82.0 %all-gather.7.cloned.1.call-done = bf16[1024,1024]{0,1:T(8,128)(2,1)} async-done(((bf16[1024,8]{0,1:T(8,128)(2,1)}), bf16[1024,1024]{0,1:T(8,128)(2,1)}) %all-gather.7.cloned.1.call-update) | async-done | bytes 2097168 | tf_op jit(solution)/shard_map/all_gather | solution.py:83
  196.1 26.4 %all-gather.9.cloned.1.call-done = bf16[512,1,1024]{2,0,1:T(8,128)(2,1)} async-done(((bf16[128,1,1024]{2,0,1:T(8,128)(2,1)}), bf16[512,1,1024]{2,0,1:T(8,128)(2,1)}) %all-gather.9.cloned.1.call-update) | async-done | bytes 1048592 | tf_op jit(solution)/shard_map/all_gather | solution.py:74
  222.5 10.1 %fusion.25 = f32[512,1024]{1,0:T(8,128)} fusion(bf16[1024,1024]{0,1:T(8,128)(2,1)} %all-gather.7.cloned.1.call-done, bf16[1024,1024]{1,0:T(8,128)(2,1)} %all-gather.5.cloned.1.call-done, bf16[512,1,1024]{2,0,1:T(8,128)(2,1)} %all-gather.9.cloned.1.call-done), kind=kOutput, calls=%fused_computation.41 | convolution fusion | flops 2181562368 | bytes 7340032 | tf_op jit(solution)/shard_map/dot_general | solution.py:81
  232.7 0.1 reshape.115
  232.8 0.4 copy.31
  233.2 0.1 copy-done.9
  233.3 0.1 broadcast_in_dim.18
  233.4 0.8 scatter_fusion
  234.2 1.2 copy.32
  235.4 34.8 %reduce-scatter.5.cloned.1.call-done = f32[128,1024]{1,0:T(8,128)} async-done(((f32[512,1024]{1,0:T(8,128)}), f32[128,1024]{1,0:T(8,128)}) %reduce-scatter.5.cloned.1.call-update) | async-done | bytes 524304 | tf_op jit(solution)/shard_map/reduce_scatter | solution.py:86
  270.2 1.3 fusion.69
  271.5 1.3 multiply_reduce_fusion
  272.8 0.9 add_convert_fusion
  (32 shorter events, 0.3 us)
Async XLA Ops:
  8.0 1.4 copy-start
  8.0 52.4 %reduce-scatter.3.cloned.1.call-start = ((), (), s32[]{:S(2)}) async-start(), calls=%async_computation.3 | async-start | bytes 2621440 | tf_op jit(solution)/shard_map/reduce_scatter | solution.py:66
  11.6 0.7 copy-start.7
  16.1 0.7 copy-start.10
  16.8 4.3 %copy-start.8 = (s32[1,1,128]{2,1,0:T(1,128)S(1)}, s32[1,1,128]{2,1,0:T(1,128)}, u32[]{:S(2)}) copy-start(s32[1,1,128]{2,1,0:T(1,128)} %param.25) | copy-start | bytes 1540
  16.8 43.6 %copy-start.2 = (bf16[512,1024]{1,0:T(8,128)(2,1)S(1)}, bf16[512,1024]{1,0:T(8,128)(2,1)}, u32[]{:S(2)}) copy-start(bf16[512,1024]{1,0:T(8,128)(2,1)} %param.14) | copy-start | bytes 3145732
  19.8 43.1 %copy-start.3 = (f32[1024]{0:T(1024)S(1)}, f32[1024]{0:T(1024)}, u32[]{:S(2)}) copy-start(f32[1024]{0:T(1024)} %param.19) | copy-start | bytes 12292
  19.8 43.1 %copy-start.4 = (f32[1024]{0:T(1024)S(1)}, f32[1024]{0:T(1024)}, u32[]{:S(2)}) copy-start(f32[1024]{0:T(1024)} %param.18) | copy-start | bytes 12292
  19.8 94.3 %all-gather.5.cloned.1.call-start = ((), (), s32[]{:S(2)}) async-start(), calls=%async_computation.4 | async-start | bytes 2113536 | tf_op jit(solution)/shard_map/all_gather | solution.py:77
  20.4 175.7 %all-gather.7.cloned.1.call-start = ((), (), s32[]{:S(2)}) async-start(), calls=%async_computation.5 | async-start | bytes 2113536 | tf_op jit(solution)/shard_map/all_gather | solution.py:83
  21.0 201.5 %all-gather.9.cloned.1.call-start = ((), (), s32[]{:S(2)}) async-start(), calls=%async_computation.7 | async-start | bytes 1310720 | tf_op jit(solution)/shard_map/all_gather | solution.py:74
  97.4 172.8 %reduce-scatter.5.cloned.1.call-start = ((), (), s32[]{:S(2)}) async-start(), calls=%async_computation.6 | async-start | bytes 2621440 | tf_op jit(solution)/shard_map/reduce_scatter | solution.py:86
  232.6 0.7 copy-start.9
  233.4 39.4 %copy-start.5 = (f32[1024]{0:T(1024)S(1)}, f32[1024]{0:T(1024)}, u32[]{:S(2)}) copy-start(f32[1024]{0:T(1024)} %param.23) | copy-start | bytes 12292
  233.4 39.4 %copy-start.6 = (f32[1024]{0:T(1024)S(1)}, f32[1024]{0:T(1024)}, u32[]{:S(2)}) copy-start(f32[1024]{0:T(1024)} %param.22) | copy-start | bytes 12292
  270.2 2.6 copy-start.1
Sparse Core Ops, SparseCore 0:
  19.9 40.4 reduce-scatter.2
  232.8 37.4 reduce-scatter.4
Sparse Core Ops, SparseCore 1:
  23.4 90.7 all-gather.4
  117.2 78.9 all-gather.6
  198.7 23.8 all-gather.8
where the time goes:
time: 282 us; the launch traced here: 281 us
  waiting for transfers between devices  200 us (71%)
  blocking collectives  30.1 us (11%)
  matrix products  18.2 us (6%)
  between operations  15.9 us (6%)
  other arithmetic  9.46 us (3%)
  local copies, waits for them, and re-layouts  7.03 us (2%)
    all_gather x1, waiting for transfers between devices, local(): lax.all_gather(down_weights, 'req', axis=1, tiled=True)  82 us
    reduce_scatter x1, waiting for transfers between devices, local(): lax.psum_scatter(partial_rows, 'grp', scatter_dimension=0, tiled=True)  39.4 us
    reduce_scatter x1, waiting for transfers between devices, local(): lax.psum_scatter(lowered_all, 'grp', scatter_dimension=0, tiled=True)  34.8 us
    all_to_all x1, blocking collectives, local(): lax.all_to_all(placed.reshape(owners, slots, width), 'req', split_axis=0,...  30.1 us
    all_gather x1, waiting for transfers between devices, local(): group_rows = lax.all_gather(even_rows, 'grp', axis=0, tiled=True)  26.4 us
    all_gather x1, waiting for transfers between devices, local(): lax.all_gather(up_weights, 'req', axis=0, tiled=True)  16.5 us
    dot_general x1, matrix products, local(): jnp.dot(activated, lax.all_gather(down_weights, 'req', axis=1, tiled=True...  10.1 us
  transfers between devices with their start and end apart: 5, of which 5 were waited for; matrix products, arithmetic and copies ran while one was open for 3% of the time, Pallas kernels for 0%

commit v1 on v0

--- a/solution.py
+++ b/solution.py
@@ -71,7 +71,9 @@
         placed.reshape(owners, slots, width), "req", split_axis=0, concat_axis=0, tiled=True
     )
     even_rows = arrived.reshape(quarter, width)
-    group_rows = lax.all_gather(even_rows, "grp", axis=0, tiled=True)
+    group_rows = jnp.concatenate(
+        lax.all_to_all(jnp.stack([even_rows] * lax.axis_size("grp")), "grp", 0, 0), axis=0
+    )
     raised = jnp.dot(
         group_rows,
         lax.all_gather(up_weights, "req", axis=0, tiled=True),

time: 282 us -> 249 us (0.88)
  waiting for transfers between devices: 200 us -> 163 us
  starting transfers between devices: 0.38 us -> 4.6 us
    all_gather x1 -> x0, waiting for transfers between devices: 26.4 us -> none  [local(): group_rows = lax.all_gather(even_rows, 'grp', axis=0, tiled=True)]
    reduce_scatter x1, waiting for transfers between devices: 34.8 us -> 28.9 us  [local(): lax.psum_scatter(lowered_all, 'grp', scatter_dimension=0, tiled=True)]
    all_gather x1, waiting for transfers between devices: 16.5 us -> 11.8 us  [local(): lax.all_gather(up_weights, 'req', axis=0, tiled=True)]
    all_to_all x0 -> x1, starting transfers between devices: none -> 4.25 us  [local(): lax.all_to_all(jnp.stack([even_rows] * lax.axis_size('grp')), 'grp', 0, 0)]
  transfers between devices with their start and end apart: 5 -> 5, of which waited for: 5 -> 4; matrix products, arithmetic and copies ran while one was open for 3% -> 4% of each run, Pallas kernels for 0% -> 0%
where the time goes in v1:
time: 249 us
  waiting for transfers between devices  163 us (65%)
  blocking collectives  30.1 us (12%)
  matrix products  18.2 us (7%)
  between operations  15.7 us (6%)
  other arithmetic  9.46 us (4%)
  local copies, waits for them, and re-layouts  7.44 us (3%)
  starting transfers between devices  4.6 us (2%)
    all_gather x1, waiting for transfers between devices, local(): lax.all_gather(down_weights, 'req', axis=1, tiled=True)  82 us
    reduce_scatter x1, waiting for transfers between devices, local(): lax.psum_scatter(partial_rows, 'grp', scatter_dimension=0, tiled=True)  39.4 us
    all_to_all x1, blocking collectives, local(): lax.all_to_all(placed.reshape(owners, slots, width), 'req', split_axis=0,...  30.1 us
    reduce_scatter x1, waiting for transfers between devices, local(): lax.psum_scatter(lowered_all, 'grp', scatter_dimension=0, tiled=True)  28.9 us
    all_gather x1, waiting for transfers between devices, local(): lax.all_gather(up_weights, 'req', axis=0, tiled=True)  11.8 us
    dot_general x1, matrix products, local(): jnp.dot(activated, lax.all_gather(down_weights, 'req', axis=1, tiled=True...  10.1 us
  transfers between devices with their start and end apart: 5, of which 4 were waited for; matrix products, arithmetic and copies ran while one was open for 4% of the time, Pallas kernels for 0%

profile of v1, /device:TPU:1, one launch (start us, length us, event | category | flops | bytes accessed | tf_op | source)
XLA Modules:
  0.0 248.8 jit_solution(9820498936093790334)
XLA Ops:
  8.1 1.3 copy-done
  9.4 2.2 fusion.101
  11.7 0.1 convert_element_type.25
  11.8 0.1 slice_bitcast_fusion
  11.9 0.5 copy-done.7
  12.3 3.7 %while.11 = (s32[]{:T(128)}, bf16[4,512,64]{1,2,0:T(8,128)(2,1)S(1)}, bf16[4,512,64]{1,2,0:T(8,128)(2,1)S(1)}, bf16[4,512,64]{1,2,0:T(8,128)(2,1)S(1)}, bf16[4,5...) while((s32[]{:T(128)}, bf16[4,512,64]{1,2,0:T(8,128)(2,1)S(1)}, ...), condition=%wide.region_3.4_spmd.clone, body=%wide.region_0.3_spmd.clone.sunk | while | flops 70024192 | bytes 3424341 | solution.py:60
  12.3 0.4 fusion.113
  12.7 0.2 fusion.114
  12.9 0.3 fusion.115
  13.3 0.4 fusion.113
  13.7 0.2 fusion.114
  13.9 0.3 fusion.115
  14.2 0.4 fusion.113
  14.6 0.2 fusion.114
  14.8 0.3 fusion.115
  15.1 0.4 fusion.113
  15.6 0.2 fusion.114
  15.8 0.3 fusion.115
  16.1 0.7 copy-done.10
  16.8 3.0 %convolution_bitcast_fusion = f32[512,1024]{1,0:T(8,128)} fusion(bf16[4,64,1024]{2,1,0:T(8,128)(2,1)} %param.17, bf16[4,512,64]{1,2,0:T(8,128)(2,1)} %copy-done.10), kind=kOutput, calls=%fused_computation.40 | convolution fusion | flops 268435456 | bytes 2883584 | tf_op jit(solution)/shard_map/nhd,hde->ne/dot_general | solution.py:63
  19.9 0.5 all-gather.3.cloned.1.call-update
  20.4 0.5 all-gather.5.cloned.1.call-update
  21.0 39.4 %reduce-scatter.3.cloned.1.call-done = f32[128,1024]{1,0:T(8,128)} async-done(((f32[512,1024]{1,0:T(8,128)}), f32[128,1024]{1,0:T(8,128)}) %reduce-scatter.3.cloned.1.call-update) | async-done | bytes 524304 | tf_op jit(solution)/shard_map/reduce_scatter | solution.py:66
  60.4 1.2 fusion.64
  61.6 1.2 multiply_reduce_fusion.1
  62.9 1.9 scatter_custom_fusion
  64.8 0.5 broadcast.107
  65.3 0.8 reduce
  66.1 0.2 reshape.130
  66.3 30.1 %all_to_all.10 = bf16[128,2,512]{2,1,0:T(2,128)(2,1)S(1)} all-to-all(bf16[128,2,512]{2,1,0:T(2,128)(2,1)S(1)} %reshape.130), channel_id=1, replica_groups=mesh['req'=128,'grp'=4] {'req'}, dimensions={0} | all-to-all | bytes 524288 | tf_op jit(solution)/shard_map/all_to_all | solution.py:70
  96.4 0.2 reshape.131
  96.6 0.1 copy.41
  96.7 1.1 stack.3
  97.8 4.3 %all-to-all-start.1 = ((bf16[4,128,1024]{2,1,0:T(8,128)(2,1)}), bf16[4,128,1024]{2,1,0:T(8,128)(2,1)}, u32[]{:S(2)}, u32[]{:S(2)}) async-start(bf16[4,128,1024]{2,1,0:T(8,128)(2,1)} %stack.3), calls=%async_computation.2 | async-start | bytes 2097152 | tf_op jit(solution)/shard_map/all_to_all | solution.py:75
  102.1 0.2 reduce-scatter.5.cloned.1.call-start
  102.3 11.8 %all-gather.3.cloned.1.call-done = bf16[1024,1024]{1,0:T(8,128)(2,1)} async-done(((bf16[8,1024]{1,0:T(8,128)(2,1)}), bf16[1024,1024]{1,0:T(8,128)(2,1)}) %all-gather.3.cloned.1.call-update) | async-done | bytes 2097168 | tf_op jit(solution)/shard_map/all_gather | solution.py:79
  114.2 82.0 %all-gather.5.cloned.1.call-done = bf16[1024,1024]{0,1:T(8,128)(2,1)} async-done(((bf16[1024,8]{0,1:T(8,128)(2,1)}), bf16[1024,1024]{0,1:T(8,128)(2,1)}) %all-gather.5.cloned.1.call-update) | async-done | bytes 2097168 | tf_op jit(solution)/shard_map/all_gather | solution.py:85
  196.1 10.1 %fusion.25 = f32[512,1024]{1,0:T(8,128)} fusion(bf16[1024,1024]{0,1:T(8,128)(2,1)} %all-gather.5.cloned.1.call-done, bf16[512,1024]{1,0:T(8,128)(2,1)} %bitcast.11, bf16[1024,1024]{1,0:T(8,128)(2,1)} %all-gather.3.cloned.1.call-done), kind=kOutput, calls=%fused_computation.41 | convolution fusion | flops 2181562368 | bytes 7340032 | tf_op jit(solution)/shard_map/dot_general | solution.py:83
  206.3 0.1 reshape.121
  206.4 0.4 copy.28
  206.8 0.1 copy-done.9
  206.9 0.1 broadcast_in_dim.18
  207.1 0.8 scatter_fusion
  207.8 1.2 copy.29
  209.0 28.9 %reduce-scatter.5.cloned.1.call-done = f32[128,1024]{1,0:T(8,128)} async-done(((f32[512,1024]{1,0:T(8,128)}), f32[128,1024]{1,0:T(8,128)}) %reduce-scatter.5.cloned.1.call-update) | async-done | bytes 524304 | tf_op jit(solution)/shard_map/reduce_scatter | solution.py:88
  237.9 1.3 fusion.63
  239.2 1.3 multiply_reduce_fusion
  240.5 0.9 add_convert_fusion
  (32 shorter events, 0.3 us)
Async XLA Ops:
  8.0 1.4 copy-start
  8.0 52.4 %reduce-scatter.3.cloned.1.call-start = ((), (), s32[]{:S(2)}) async-start(), calls=%async_computation.4 | async-start | bytes 2621440 | tf_op jit(solution)/shard_map/reduce_scatter | solution.py:66
  11.6 0.7 copy-start.7
  16.1 0.7 copy-start.10
  16.8 4.2 %copy-start.8 = (s32[1,1,128]{2,1,0:T(1,128)S(1)}, s32[1,1,128]{2,1,0:T(1,128)}, u32[]{:S(2)}) copy-start(s32[1,1,128]{2,1,0:T(1,128)} %param.25) | copy-start | bytes 1540
  16.8 43.6 %copy-start.2 = (bf16[512,1024]{1,0:T(8,128)(2,1)S(1)}, bf16[512,1024]{1,0:T(8,128)(2,1)}, u32[]{:S(2)}) copy-start(bf16[512,1024]{1,0:T(8,128)(2,1)} %param.14) | copy-start | bytes 3145732
  19.8 43.1 %copy-start.3 = (f32[1024]{0:T(1024)S(1)}, f32[1024]{0:T(1024)}, u32[]{:S(2)}) copy-start(f32[1024]{0:T(1024)} %param.19) | copy-start | bytes 12292
  19.8 43.1 %copy-start.4 = (f32[1024]{0:T(1024)S(1)}, f32[1024]{0:T(1024)}, u32[]{:S(2)}) copy-start(f32[1024]{0:T(1024)} %param.18) | copy-start | bytes 12292
  19.8 94.4 %all-gather.3.cloned.1.call-start = ((), (), s32[]{:S(2)}) async-start(), calls=%async_computation.5 | async-start | bytes 2113536 | tf_op jit(solution)/shard_map/all_gather | solution.py:79
  20.4 175.7 %all-gather.5.cloned.1.call-start = ((), (), s32[]{:S(2)}) async-start(), calls=%async_computation.6 | async-start | bytes 2113536 | tf_op jit(solution)/shard_map/all_gather | solution.py:85
  97.8 98.3 %all-to-all-start.1 = ((bf16[4,128,1024]{2,1,0:T(8,128)(2,1)}), bf16[4,128,1024]{2,1,0:T(8,128)(2,1)}, u32[]{:S(2)}, u32[]{:S(2)}) async-start(bf16[4,128,1024]{2,1,0:T(8,128)(2,1)} %stack.3), calls=%async_computation.2 | async-start | bytes 2097152 | tf_op jit(solution)/shard_map/all_to_all | solution.py:75
  102.1 135.8 %reduce-scatter.5.cloned.1.call-start = ((), (), s32[]{:S(2)}) async-start(), calls=%async_computation.7 | async-start | bytes 2621440 | tf_op jit(solution)/shard_map/reduce_scatter | solution.py:88
  206.3 0.7 copy-start.9
  207.0 33.5 %copy-start.5 = (f32[1024]{0:T(1024)S(1)}, f32[1024]{0:T(1024)}, u32[]{:S(2)}) copy-start(f32[1024]{0:T(1024)} %param.23) | copy-start | bytes 12292
  207.0 33.5 %copy-start.6 = (f32[1024]{0:T(1024)S(1)}, f32[1024]{0:T(1024)}, u32[]{:S(2)}) copy-start(f32[1024]{0:T(1024)} %param.22) | copy-start | bytes 12292
  237.9 2.6 %copy-start.1 = (f32[128,1024]{1,0:T(8,128)S(1)}, f32[128,1024]{1,0:T(8,128)}, u32[]{:S(2)}) copy-start(f32[128,1024]{1,0:T(8,128)} %reduce-scatter.5.cloned.1.call-done) | copy-start | bytes 1572868
Sparse Core Ops, SparseCore 0:
  19.9 40.4 reduce-scatter.2
  206.4 31.4 reduce-scatter.4
Sparse Core Ops, SparseCore 1:
  23.4 90.7 all-gather.2
  117.2 78.9 all-gather.4
